TPU v7x, 32 devices: a whole 2x2x4 slice. The times are simulated.
32 devices in a mesh: batch: 4 (over z), seq: 8 (over y, x, core).
Axes of the slice: x: 2, y: 2, z: 4, core: 2. Of those that a mesh axis runs over, the one named last changes fastest.
Arguments:
- block_input: bfloat16 [16384, 768], P(('batch', 'seq')), may hold values from -6 to 6
- history: bfloat16 [8, 16384, 768], P(None, ('batch', 'seq')), may hold values from -6 to 6
- cotangent: bfloat16 [16384, 768], P(('batch', 'seq')), may hold values from -6 to 6
- qkv_weight: bfloat16 [768, 2304], P('batch', 'seq'), may hold values from -0.21875 to 0.21875
- proj_weight: bfloat16 [768, 768], P('batch', 'seq'), may hold values from -1.25 to 1.25
- up_weight: bfloat16 [768, 3072], P('batch', 'seq'), may hold values from -0.21875 to 0.21875
- down_weight: bfloat16 [3072, 768], P('batch', 'seq'), may hold values from -0.109375 to 0.109375
- norm1_gain: float32 [768], replicated, may hold values from 0.5 to 1.5
- norm1_bias: float32 [768], replicated, may hold values from -1.2 to 1.2
- norm2_gain: float32 [768], replicated, may hold values from 0.5 to 1.5
- norm2_bias: float32 [768], replicated, may hold values from -1.2 to 1.2
- dwa_weights: float32 [9], replicated, may hold values from 0.3 to 1
- pair_order: int32 [4, 24], P('batch'), may hold values from 0 to 23, each once within a row
- long_group: int32 [4, 2], P('batch'), may hold values from 0 to 2
Outputs:
- block_output: bfloat16 [16384, 768], P(('batch', 'seq'))
- input_grad: bfloat16 [16384, 768], P(('batch', 'seq'))
- history_grad: bfloat16 [8, 16384, 768], P(None, ('batch', 'seq'))
- row_lse: float32 [4, 24, 2048], P('batch', 'seq')
- qkv_grad: float32 [768, 2304], P('batch', 'seq')
- proj_grad: float32 [768, 768], P('batch', 'seq')
- up_grad: float32 [768, 3072], P('batch', 'seq')
- down_grad: float32 [3072, 768], P('batch', 'seq')
- norm1_gain_grad: float32 [768], replicated
- norm1_bias_grad: float32 [768], replicated
- norm2_gain_grad: float32 [768], replicated
- norm2_bias_grad: float32 [768], replicated
- dwa_grad: float32 [9], replicated
Inputs may be any that keep to these rules, and one draw needn't show every extreme that they name: `pair_order`: each row lists each of its group's 24 pairs once. `long_group`: an entry v: that slot holds 2^v sequences of 2048 // 2^v tokens.
All inputs are finite; a program needn't handle non-finite values.
Results may differ from a plain program's by a relative error of at most 0.017.
Values may be sent and summed in bfloat16 or wider, within the bound.
No kernel may reach another device: no remote copies, remote signals or barrier semaphores. Data moves between devices by JAX's collectives and lax.ppermute only.
A program may use at most 192 MiB of HBM per device.

v0:
```python
import jax
import jax.numpy as jnp
from jax import lax
from jax.sharding import PartitionSpec as P

D = 768
HEADS = 12
HD = 64
SLOT = 2048
HIST = 8
NORM_EPS = 1e-05
MASKED = -1e30


def norm_rows(values, gain, shift):
    row_mean = jnp.mean(values, axis=-1, keepdims=True)
    centred = values - row_mean
    variance = jnp.mean(centred * centred, axis=-1, keepdims=True)
    inv_std = lax.rsqrt(variance + NORM_EPS)
    normed = centred * inv_std
    return (normed * gain + shift, normed, inv_std)


def norm_back(grad_in, normed, inv_std, gain):
    scaled = grad_in * gain
    centred = (
        scaled
        - jnp.mean(scaled, axis=-1, keepdims=True)
        - normed * jnp.mean(scaled * normed, axis=-1, keepdims=True)
    )
    return (centred * inv_std, jnp.sum(grad_in * normed, axis=0), jnp.sum(grad_in, axis=0))


def rotate(values, cosine, sine_tab):
    half_size = values.shape[-1] // 2
    front = values[..., :half_size]
    behind = values[..., half_size:]
    cos_part = cosine[..., None, :]
    sin_part = sine_tab[..., None, :]
    return jnp.concatenate(
        [front * cos_part - behind * sin_part, behind * cos_part + front * sin_part], axis=-1
    )


def unrotate(values, cosine, sine_tab):
    half_size = values.shape[-1] // 2
    front = values[..., :half_size]
    behind = values[..., half_size:]
    cos_part = cosine[..., None, :]
    sin_part = sine_tab[..., None, :]
    return jnp.concatenate(
        [front * cos_part + behind * sin_part, behind * cos_part - front * sin_part], axis=-1
    )


def to_pairs(stacked, order_row, n_seq, per_dev):
    slot_count, piece_len, part_count, head_count, head_size = stacked.shape
    reordered = jnp.transpose(stacked, (0, 3, 2, 1, 4)).reshape(
        slot_count * head_count, part_count, piece_len * head_size
    )
    return jnp.take(reordered, order_row, axis=0).reshape(
        n_seq, per_dev, part_count, piece_len * head_size
    )


def pairs_whole(incoming, head_size):
    n_seq, per_dev, part_count, flat_len = incoming.shape
    piece_len = flat_len // head_size
    reordered = jnp.transpose(
        incoming.reshape(n_seq, per_dev, part_count, piece_len, head_size), (1, 2, 0, 3, 4)
    )
    return reordered.reshape(per_dev, part_count, n_seq * piece_len, head_size)


def pairs_split(whole_seq, n_seq):
    per_dev, part_count, seq_len, head_size = whole_seq.shape
    return jnp.transpose(
        whole_seq.reshape(per_dev, part_count, n_seq, seq_len // n_seq * head_size), (2, 0, 1, 3)
    )


def tokens_back(incoming, inverse, slot_count, head_size):
    n_seq, per_dev, part_count, flat_len = incoming.shape
    piece_len = flat_len // head_size
    ordered = jnp.take(incoming.reshape(n_seq * per_dev, part_count, flat_len), inverse, axis=0)
    head_count = n_seq * per_dev // slot_count
    return jnp.transpose(
        ordered.reshape(slot_count, head_count, part_count, piece_len, head_size), (0, 3, 2, 1, 4)
    )


def local(
    block_input,
    history,
    cotangent,
    qkv_weight,
    proj_weight,
    up_weight,
    down_weight,
    norm1_gain,
    norm1_bias,
    norm2_gain,
    norm2_bias,
    dwa_weights,
    pair_order,
    long_group,
):
    n_seq = lax.axis_size("seq")
    row_count = block_input.shape[0]
    piece_len = SLOT // n_seq
    slot_count = row_count // piece_len
    pair_count = slot_count * HEADS
    per_dev = pair_count // n_seq
    block_rows = min(512, SLOT)
    block_count = SLOT // block_rows
    score_scale = HD ** (-0.5)
    slot_flags = long_group[0]
    seg_len = SLOT // jnp.left_shift(jnp.ones_like(slot_flags), slot_flags)
    position = jnp.arange(SLOT, dtype=jnp.int32)
    segment_all = position[None, :] // seg_len[:, None]
    doc_place = (position[None, :] % seg_len[:, None]).astype(jnp.float32)
    frequency = jnp.power(10000.0, jnp.arange(HD // 2, dtype=jnp.float32) * (-2.0 / HD))
    angles = doc_place[..., None] * frequency
    my_index = lax.axis_index("seq")
    my_start = my_index * piece_len
    cosine = lax.dynamic_slice_in_dim(jnp.cos(angles), my_start, piece_len, 1)
    sine_tab = lax.dynamic_slice_in_dim(jnp.sin(angles), my_start, piece_len, 1)
    order_row = pair_order[0]
    inverse = (
        jnp.zeros((pair_count,), jnp.int32)
        .at[order_row]
        .set(jnp.arange(pair_count, dtype=jnp.int32))
    )
    held_pairs = lax.dynamic_slice_in_dim(order_row, my_index * per_dev, per_dev, 0)
    pair_segment = jnp.take(segment_all, held_pairs // HEADS, axis=0)
    row_parts = (
        lax.all_gather(qkv_weight, "batch", axis=0, tiled=True),
        lax.all_gather(proj_weight, "batch", axis=0, tiled=True),
        lax.all_gather(up_weight, "batch", axis=0, tiled=True),
        lax.all_gather(down_weight, "batch", axis=0, tiled=True),
    )
    w_qkv, w_proj, w_up, w_down = (
        lax.all_gather(row_parts[0], "seq", axis=1, tiled=True),
        lax.all_gather(row_parts[1], "seq", axis=1, tiled=True),
        lax.all_gather(row_parts[2], "seq", axis=1, tiled=True),
        lax.all_gather(row_parts[3], "seq", axis=1, tiled=True),
    )
    inputs32 = block_input.astype(jnp.float32)
    norm1_out, normed1, inv_std1 = norm_rows(inputs32, norm1_gain, norm1_bias)
    norm1_low = norm1_out.astype(jnp.bfloat16)
    qkv_out = jnp.dot(norm1_low, w_qkv, preferred_element_type=jnp.float32)
    queries = rotate(qkv_out[:, :D].reshape(slot_count, piece_len, HEADS, HD), cosine, sine_tab)
    keys_rot = rotate(
        qkv_out[:, D : 2 * D].reshape(slot_count, piece_len, HEADS, HD), cosine, sine_tab
    )
    values_in = qkv_out[:, 2 * D :].reshape(slot_count, piece_len, HEADS, HD)
    stacked = jnp.stack([queries, keys_rot, values_in], axis=2).astype(jnp.bfloat16)
    incoming = lax.all_to_all(
        to_pairs(stacked, order_row, n_seq, per_dev), "seq", split_axis=0, concat_axis=0, tiled=True
    )
    sequences = pairs_whole(incoming, HD)
    query_pairs = sequences[:, 0]
    key_pairs = sequences[:, 1]
    value_pairs = sequences[:, 2]

    def masked_scores(start_row, query_block):
        raw_scores = jnp.einsum(
            "pqd,pkd->pqk", query_block, key_pairs, preferred_element_type=jnp.float32
        )
        query_place = start_row + jnp.arange(block_rows, dtype=jnp.int32)
        query_seg = lax.dynamic_slice_in_dim(pair_segment, start_row, block_rows, 1)
        allowed = (position[None, None, :] <= query_place[None, :, None]) & (
            pair_segment[:, None, :] == query_seg[:, :, None]
        )
        return jnp.where(allowed, raw_scores * score_scale, MASKED)

    def forward_block(start_row):
        query_block = lax.dynamic_slice_in_dim(query_pairs, start_row, block_rows, 1)
        scores = masked_scores(start_row, query_block)
        row_top = jnp.max(scores, axis=-1, keepdims=True)
        weights_exp = jnp.exp(scores - row_top)
        row_total = jnp.sum(weights_exp, axis=-1, keepdims=True)
        probability = (weights_exp / row_total).astype(jnp.bfloat16)
        attn_block = jnp.einsum(
            "pqk,pkd->pqd", probability, value_pairs, preferred_element_type=jnp.float32
        ).astype(jnp.bfloat16)
        return (attn_block, row_top[..., 0] + jnp.log(row_total[..., 0]))

    starts = jnp.arange(block_count, dtype=jnp.int32) * block_rows
    attn_blocks, totals = lax.map(forward_block, starts)
    attended_pairs = jnp.transpose(attn_blocks, (1, 0, 2, 3)).reshape(per_dev, 1, SLOT, HD)
    log_total = jnp.transpose(totals, (1, 0, 2)).reshape(per_dev, SLOT)
    returned = lax.all_to_all(
        pairs_split(attended_pairs, n_seq), "seq", split_axis=0, concat_axis=0, tiled=True
    )
    attended = tokens_back(returned, inverse, slot_count, HD).reshape(row_count, D)
    middle = inputs32 + jnp.dot(attended, w_proj, preferred_element_type=jnp.float32)
    norm2_out, normed2, inv_std2 = norm_rows(middle, norm2_gain, norm2_bias)
    norm2_low = norm2_out.astype(jnp.bfloat16)
    hidden_up = jnp.dot(norm2_low, w_up, preferred_element_type=jnp.float32)
    gelu_out, gelu_pull = jax.vjp(lambda hidden: jax.nn.gelu(hidden, approximate=True), hidden_up)
    gelu_low = gelu_out.astype(jnp.bfloat16)
    block_out = middle + jnp.dot(gelu_low, w_down, preferred_element_type=jnp.float32)
    dwa_out = dwa_weights[HIST] * block_out
    for layer_idx in range(HIST):
        dwa_out = dwa_out + dwa_weights[layer_idx] * history[layer_idx].astype(jnp.float32)
    block_output = dwa_out.astype(jnp.bfloat16)
    grad_out = cotangent.astype(jnp.float32)
    history_grad = (dwa_weights[:HIST, None, None] * grad_out[None]).astype(jnp.bfloat16)
    dwa_terms = [
        jnp.sum(history[layer_idx].astype(jnp.float32) * grad_out) for layer_idx in range(HIST)
    ]
    dwa_terms.append(jnp.sum(block_out * grad_out))
    dwa_local = jnp.stack(dwa_terms)
    again_parts = (
        lax.all_gather(qkv_weight, "batch", axis=0, tiled=True),
        lax.all_gather(proj_weight, "batch", axis=0, tiled=True),
        lax.all_gather(up_weight, "batch", axis=0, tiled=True),
        lax.all_gather(down_weight, "batch", axis=0, tiled=True),
    )
    w_qkv, w_proj, w_up, w_down = (
        lax.all_gather(again_parts[0], "seq", axis=1, tiled=True),
        lax.all_gather(again_parts[1], "seq", axis=1, tiled=True),
        lax.all_gather(again_parts[2], "seq", axis=1, tiled=True),
        lax.all_gather(again_parts[3], "seq", axis=1, tiled=True),
    )
    dy_full = dwa_weights[HIST] * grad_out
    dmlp_low = dy_full.astype(jnp.bfloat16)
    down_local = jnp.einsum("nf,nd->fd", gelu_low, dmlp_low, preferred_element_type=jnp.float32)
    dgelu = jnp.einsum("nd,fd->nf", dmlp_low, w_down, preferred_element_type=jnp.float32)
    dup_low = gelu_pull(dgelu)[0].astype(jnp.bfloat16)
    up_local = jnp.einsum("nd,nf->df", norm2_low, dup_low, preferred_element_type=jnp.float32)
    dnorm2 = jnp.einsum("nf,df->nd", dup_low, w_up, preferred_element_type=jnp.float32)
    dmid_norm, gain2_local, bias2_local = norm_back(dnorm2, normed2, inv_std2, norm2_gain)
    dmiddle = dy_full + dmid_norm
    dmiddle_low = dmiddle.astype(jnp.bfloat16)
    proj_local = jnp.einsum("nd,ne->de", attended, dmiddle_low, preferred_element_type=jnp.float32)
    dattended = jnp.einsum(
        "ne,de->nd", dmiddle_low, w_proj, preferred_element_type=jnp.float32
    ).astype(jnp.bfloat16)
    dattn_tokens = dattended.reshape(slot_count, piece_len, 1, HEADS, HD)
    dattn_in = lax.all_to_all(
        to_pairs(dattn_tokens, order_row, n_seq, per_dev),
        "seq",
        split_axis=0,
        concat_axis=0,
        tiled=True,
    )
    dout_pairs = pairs_whole(dattn_in, HD)[:, 0]

    def backward_block(sums_carry, start_row):
        dkeys_sum, dvalues_sum = sums_carry
        query_block = lax.dynamic_slice_in_dim(query_pairs, start_row, block_rows, 1)
        dout_block = lax.dynamic_slice_in_dim(dout_pairs, start_row, block_rows, 1)
        total_block = lax.dynamic_slice_in_dim(log_total, start_row, block_rows, 1)
        probability = jnp.exp(masked_scores(start_row, query_block) - total_block[..., None])
        prob_low = probability.astype(jnp.bfloat16)
        dprob_full = jnp.einsum(
            "pqd,pkd->pqk", dout_block, value_pairs, preferred_element_type=jnp.float32
        )
        row_delta = jnp.sum(probability * dprob_full, axis=-1, keepdims=True)
        dscore = (probability * (dprob_full - row_delta) * score_scale).astype(jnp.bfloat16)
        dquery_block = jnp.einsum(
            "pqk,pkd->pqd", dscore, key_pairs, preferred_element_type=jnp.float32
        )
        dkeys_sum = dkeys_sum + jnp.einsum(
            "pqk,pqd->pkd", dscore, query_block, preferred_element_type=jnp.float32
        )
        dvalues_sum = dvalues_sum + jnp.einsum(
            "pqk,pqd->pkd", prob_low, dout_block, preferred_element_type=jnp.float32
        )
        return ((dkeys_sum, dvalues_sum), dquery_block)

    zero_pairs = jnp.zeros((per_dev, SLOT, HD), jnp.float32)
    (dkeys_sum, dvalues_sum), dquery_blocks = lax.scan(
        backward_block, (zero_pairs, zero_pairs), starts
    )
    dquery = jnp.transpose(dquery_blocks, (1, 0, 2, 3)).reshape(per_dev, SLOT, HD)
    dpairs = jnp.stack([dquery, dkeys_sum, dvalues_sum], axis=1).astype(jnp.bfloat16)
    dreturned = lax.all_to_all(
        pairs_split(dpairs, n_seq), "seq", split_axis=0, concat_axis=0, tiled=True
    )
    dtokens = tokens_back(dreturned, inverse, slot_count, HD)
    dq_rows = unrotate(dtokens[:, :, 0].astype(jnp.float32), cosine, sine_tab).reshape(row_count, D)
    dk_rows = unrotate(dtokens[:, :, 1].astype(jnp.float32), cosine, sine_tab).reshape(row_count, D)
    dv_rows = dtokens[:, :, 2].astype(jnp.float32).reshape(row_count, D)
    dqkv_low = jnp.concatenate([dq_rows, dk_rows, dv_rows], axis=-1).astype(jnp.bfloat16)
    qkv_local = jnp.einsum("nd,nf->df", norm1_low, dqkv_low, preferred_element_type=jnp.float32)
    dnorm1 = jnp.einsum("nf,df->nd", dqkv_low, w_qkv, preferred_element_type=jnp.float32)
    dinput_norm, gain1_local, bias1_local = norm_back(dnorm1, normed1, inv_std1, norm1_gain)
    input_grad = (dmiddle + dinput_norm).astype(jnp.bfloat16)
    col_sums = (
        lax.psum_scatter(
            qkv_local.astype(jnp.bfloat16), "seq", scatter_dimension=1, tiled=True
        ).astype(jnp.float32),
        lax.psum_scatter(
            proj_local.astype(jnp.bfloat16), "seq", scatter_dimension=1, tiled=True
        ).astype(jnp.float32),
        lax.psum_scatter(
            up_local.astype(jnp.bfloat16), "seq", scatter_dimension=1, tiled=True
        ).astype(jnp.float32),
        lax.psum_scatter(
            down_local.astype(jnp.bfloat16), "seq", scatter_dimension=1, tiled=True
        ).astype(jnp.float32),
    )
    qkv_grad, proj_grad, up_grad, down_grad = (
        lax.psum_scatter(
            col_sums[0].astype(jnp.bfloat16), "batch", scatter_dimension=0, tiled=True
        ).astype(jnp.float32),
        lax.psum_scatter(
            col_sums[1].astype(jnp.bfloat16), "batch", scatter_dimension=0, tiled=True
        ).astype(jnp.float32),
        lax.psum_scatter(
            col_sums[2].astype(jnp.bfloat16), "batch", scatter_dimension=0, tiled=True
        ).astype(jnp.float32),
        lax.psum_scatter(
            col_sums[3].astype(jnp.bfloat16), "batch", scatter_dimension=0, tiled=True
        ).astype(jnp.float32),
    )
    gain1_grad, bias1_grad, gain2_grad, bias2_grad, dwa_grad = lax.psum(
        (gain1_local, bias1_local, gain2_local, bias2_local, dwa_local), ("batch", "seq")
    )
    row_lse = log_total.reshape(1, per_dev, SLOT)
    return (
        block_output,
        input_grad,
        history_grad,
        row_lse,
        qkv_grad,
        proj_grad,
        up_grad,
        down_grad,
        gain1_grad,
        bias1_grad,
        gain2_grad,
        bias2_grad,
        dwa_grad,
    )


def solution(mesh):
    placed = (
        P(("batch", "seq"), None),
        P(None, ("batch", "seq"), None),
        P(("batch", "seq"), None),
        P("batch", "seq"),
        P("batch", "seq"),
        P("batch", "seq"),
        P("batch", "seq"),
        P(),
        P(),
        P(),
        P(),
        P(),
        P("batch", None),
        P("batch", None),
    )
    return jax.shard_map(
        local,
        mesh=mesh,
        in_specs=placed,
        out_specs=(
            P(("batch", "seq"), None),
            P(("batch", "seq"), None),
            P(None, ("batch", "seq"), None),
            P("batch", "seq", None),
            P("batch", "seq"),
            P("batch", "seq"),
            P("batch", "seq"),
            P("batch", "seq"),
            P(),
            P(),
            P(),
            P(),
            P(),
        ),
        check_vma=False,
    )
```

profile of v0, /device:TPU:0, one launch (start us, length us, event | category | flops | bytes accessed | tf_op | source)
XLA Modules:
  0.0 866.0 jit_solution(16337869639670817424)
XLA Ops:
  7.3 18.6 %all_gather.32 = bf16[768,288]{1,0:T(8,128)(2,1)S(1)} all-gather(bf16[192,288]{1,0:T(8,128)(2,1)} %param.25), channel_id=1, replica_groups=mesh['batch'=4,'seq'=8] {'batch'}, dimensions={0}, use_global_device_ids=true | all-gather | bytes 552960 | tf_op jit(solution)/shard_map/all_gather | solution.py:137
  27.0 13.8 %all_gather.34 = bf16[768,96]{1,0:T(8,128)(2,1)S(1)} all-gather(bf16[192,96]{1,0:T(8,128)(2,1)} %param.26), channel_id=1, replica_groups=mesh['batch'=4,'seq'=8] {'batch'}, dimensions={0}, use_global_device_ids=true | all-gather | bytes 184320 | tf_op jit(solution)/shard_map/all_gather | solution.py:138
  41.7 17.0 %all_gather.36 = bf16[768,384]{1,0:T(8,128)(2,1)} all-gather(bf16[192,384]{1,0:T(8,128)(2,1)S(1)} %copy-done.18), channel_id=1, replica_groups=mesh['batch'=4,'seq'=8] {'batch'}, dimensions={0}, use_global_device_ids=true | all-gather | bytes 737280 | tf_op jit(solution)/shard_map/all_gather | solution.py:139
  91.2 8.2 reshape.607
  99.4 7.2 gather_fusion.1
  116.1 17.4 %all_gather.38 = bf16[3072,96]{0,1:T(8,128)(2,1)} all-gather(bf16[768,96]{0,1:T(8,128)(2,1)S(1)} %copy-done.19), channel_id=1, replica_groups=mesh['batch'=4,'seq'=8] {'batch'}, dimensions={0}, use_global_device_ids=true | all-gather | bytes 737280 | tf_op jit(solution)/shard_map/all_gather | solution.py:140
  134.2 27.8 %all-to-all-done = bf16[8,3,3,16384]{3,1,2,0:T(4,128)(2,1)S(1)} async-done(((bf16[8,3,3,16384]{3,1,2,0:T(4,128)(2,1)}), bf16[8,3,3,16384]{3,1,2,0:T(4,128)(2,1)S(1)}, u32[]{:S(2)}, u32[]{:S(2)}) %all-to-all-start) | async-done | bytes 2359328 | tf_op jit(solution)/shard_map/all_to_all | solution.py:158
  165.2 7.1 reshape.515
  181.9 80.8 %while.28 = (s32[]{:T(128)}, bf16[4,3,512,64]{2,3,1,0:T(8,128)(2,1)}, f32[4,3,512]{2,1,0:T(4,128)S(1)}, s32[4]{0:T(128)S(1)}, s32[3,2048]{1,0:T(4,128)S(1)}, /*i...) while((s32[]{:T(128)}, ...), condition=%wide.region_5.7_spmd.clone, body=%wide.region_2.6_spmd.clone.sunk | while | flops 863075328 | bytes 44073140 | solution.py:190
  185.8 5.5 fusion.157
  196.3 5.8 fusion.159
  216.5 5.8 fusion.159
  236.7 5.8 fusion.159
  256.9 5.8 fusion.159
  273.7 13.8 %all-to-all-done.1 = bf16[8,3,1,16384]{3,1,2,0:T(4,128)(2,1)S(1)} async-done(((bf16[8,3,1,16384]{3,1,2,0:T(4,128)(2,1)}), bf16[8,3,1,16384]{3,1,2,0:T(4,128)(2,1)S(1)}, u32[]{:S(2)}, u32[]{:S(2)}) %all-to-all-start.1) | async-done | bytes 786464 | tf_op jit(solution)/shard_map/all_to_all | solution.py:193
  298.1 7.1 fusion.111
  305.2 10.1 %fusion.58 = bf16[512,3072]{1,0:T(8,128)(2,1)S(1)} fusion(f32[512,3072]{1,0:T(8,128)} %fusion.111, bf16[3072,768]{0,1:T(8,128)(2,1)} %all-gather.11.cloned.1.call-done, bf16[512,768]{1,0:T(8,128)(2,1)S(1)} %copy-done.9, f32[]{:T(128)} %bitcast), kind=kOutput, calls=%fused_computation.65 | convolution fusion | flops 2448556032 | bytes 14942212 | tf_op jit(solution)/shard_map/nd,fd->nf/dot_general | solution.py:230
  318.9 15.2 %fusion.84 = (bf16[512,768]{1,0:T(8,128)(2,1)}, f32[512,768]{1,0:T(8,128)S(1)}) fusion(f32[]{:T(128)} %bitcast.39, f32[]{:T(128)} %bitcast.37, f32[]{:T(128)} %bitcast.35, f32[]{:T(128)} %bitcast.33, f32[]{:T(128)} %bitcast.31, f32[]{:T(128)} %bitcast.29, f32[]{:T(128)} %bitcast.27, f32[]{:T(128)} %bitcast.25, f32[]{:T(128)} %bitcast, ...), kind=kOutput, calls=%fused_computation.120 | convolution fusion | flops 2440691712 | bytes 21233700 | tf_op jit(solution)/shard_map/dot_general | solution.py:203
  341.1 6.5 convolution_convert_fusion.2
  347.5 6.7 copy.156
  374.5 8.8 %convolution_convert_fusion.1 = bf16[3072,768]{0,1:T(8,128)(2,1)} fusion(bf16[512,768]{1,0:T(8,128)(2,1)} %param.24, f32[]{:T(128)} %bitcast, f32[512,3072]{1,0:T(8,128)} %fusion.111), kind=kOutput, calls=%fused_computation.68 | convolution fusion | flops 2433613824 | bytes 11796484 | tf_op jit(solution)/shard_map/nf,nd->fd/dot_general | solution.py:229
  383.4 6.4 all-to-all-done.2
  396.4 239.9 %while.29 = (s32[]{:T(128)}, f32[3,2048,64]{1,2,0:T(8,128)}, f32[3,2048,64]{1,2,0:T(8,128)S(1)}, bf16[4,3,512,64]{2,3,1,0:T(8,128)(2,1)}, s32[4]{0:T(128)S(1)}, ...) while((s32[]{:T(128)}, f32[3,2048,64]{1,2,0:T(8,128)}, ...), condition=%wide.region_13.16_spmd.clone, body=%wide.region_11.15_spmd.clone.sunk | while | flops 2066226688 | bytes 200737024 | solution.py:275
  400.6 6.1 subtract_exponential_fusion.3
  411.3 6.4 fusion.170
  417.7 18.6 %fusion.173 = bf16[4,3,512,64]{2,3,1,0:T(8,128)(2,1)} fusion(bf16[4,3,512,64]{2,3,1,0:T(8,128)(2,1)} %get-tuple-element.576, s32[]{:T(128)S(6)} %copy.183, bf16[3,2048,64]{1,2,0:T(8,128)(2,1)} %get-tuple-element.594, f32[3,512,2048]{2,1,0:T(8,128)} %copy-done, f32[3,512,2048]{2,1,0:T(8,128)} %fusion.170), kind=kOutput, calls=%fused_computation.39.clone.1 | convolution fusion | flops 418385408 | bytes 51511300 | tf_op jit(solution)/shard_map/while/body/eval_jaxpr/pqk,pkd->pqd/dot_general | solution.py:263
  436.3 22.0 %fusion.171 = f32[3,2048,64]{1,2,0:T(8,128)} fusion(f32[3,512,2048]{2,1,0:T(8,128)} %copy-done, f32[3,512,2048]{2,1,0:T(8,128)} %fusion.170, f32[3,2048,64]{1,2,0:T(8,128)} %get-tuple-element.574, pred[]{:T(512)S(6)} %compare.3, bf16[3,2048,64]{1,2,0:T(8,128)(2,1)} %get-tuple-element.593, s32[]{:T(128)S(6)} %select_n.227), kind=kOutput, calls=%fused_computation.37.clone.1 | convolution fusion | flops 419171840 | bytes 53673988 | tf_op jit(solution)/shard_map/while/body/eval_jaxpr/pqk,pqd->pkd/dot_general | solution.py:266
  462.2 6.1 subtract_exponential_fusion.3
  472.9 6.4 fusion.170
  479.3 18.5 %fusion.173 = bf16[4,3,512,64]{2,3,1,0:T(8,128)(2,1)} fusion(bf16[4,3,512,64]{2,3,1,0:T(8,128)(2,1)} %get-tuple-element.576, s32[]{:T(128)S(6)} %copy.183, bf16[3,2048,64]{1,2,0:T(8,128)(2,1)} %get-tuple-element.594, f32[3,512,2048]{2,1,0:T(8,128)} %copy-done, f32[3,512,2048]{2,1,0:T(8,128)} %fusion.170), kind=kOutput, calls=%fused_computation.39.clone.1 | convolution fusion | flops 418385408 | bytes 51511300 | tf_op jit(solution)/shard_map/while/body/eval_jaxpr/pqk,pkd->pqd/dot_general | solution.py:263
  497.8 20.1 %fusion.171 = f32[3,2048,64]{1,2,0:T(8,128)} fusion(f32[3,512,2048]{2,1,0:T(8,128)} %copy-done, f32[3,512,2048]{2,1,0:T(8,128)} %fusion.170, f32[3,2048,64]{1,2,0:T(8,128)} %get-tuple-element.574, pred[]{:T(512)S(6)} %compare.3, bf16[3,2048,64]{1,2,0:T(8,128)(2,1)} %get-tuple-element.593, s32[]{:T(128)S(6)} %select_n.227), kind=kOutput, calls=%fused_computation.37.clone.1 | convolution fusion | flops 419171840 | bytes 53673988 | tf_op jit(solution)/shard_map/while/body/eval_jaxpr/pqk,pqd->pkd/dot_general | solution.py:266
  521.9 6.1 subtract_exponential_fusion.3
  532.5 6.4 fusion.170
  538.9 17.9 %fusion.173 = bf16[4,3,512,64]{2,3,1,0:T(8,128)(2,1)} fusion(bf16[4,3,512,64]{2,3,1,0:T(8,128)(2,1)} %get-tuple-element.576, s32[]{:T(128)S(6)} %copy.183, bf16[3,2048,64]{1,2,0:T(8,128)(2,1)} %get-tuple-element.594, f32[3,512,2048]{2,1,0:T(8,128)} %copy-done, f32[3,512,2048]{2,1,0:T(8,128)} %fusion.170), kind=kOutput, calls=%fused_computation.39.clone.1 | convolution fusion | flops 418385408 | bytes 51511300 | tf_op jit(solution)/shard_map/while/body/eval_jaxpr/pqk,pkd->pqd/dot_general | solution.py:263
  556.8 20.1 %fusion.171 = f32[3,2048,64]{1,2,0:T(8,128)} fusion(f32[3,512,2048]{2,1,0:T(8,128)} %copy-done, f32[3,512,2048]{2,1,0:T(8,128)} %fusion.170, f32[3,2048,64]{1,2,0:T(8,128)} %get-tuple-element.574, pred[]{:T(512)S(6)} %compare.3, bf16[3,2048,64]{1,2,0:T(8,128)(2,1)} %get-tuple-element.593, s32[]{:T(128)S(6)} %select_n.227), kind=kOutput, calls=%fused_computation.37.clone.1 | convolution fusion | flops 419171840 | bytes 53673988 | tf_op jit(solution)/shard_map/while/body/eval_jaxpr/pqk,pqd->pkd/dot_general | solution.py:266
  580.9 6.1 subtract_exponential_fusion.3
  591.6 6.4 fusion.170
  598.0 17.9 %fusion.173 = bf16[4,3,512,64]{2,3,1,0:T(8,128)(2,1)} fusion(bf16[4,3,512,64]{2,3,1,0:T(8,128)(2,1)} %get-tuple-element.576, s32[]{:T(128)S(6)} %copy.183, bf16[3,2048,64]{1,2,0:T(8,128)(2,1)} %get-tuple-element.594, f32[3,512,2048]{2,1,0:T(8,128)} %copy-done, f32[3,512,2048]{2,1,0:T(8,128)} %fusion.170), kind=kOutput, calls=%fused_computation.39.clone.1 | convolution fusion | flops 418385408 | bytes 51511300 | tf_op jit(solution)/shard_map/while/body/eval_jaxpr/pqk,pkd->pqd/dot_general | solution.py:263
  615.9 20.0 %fusion.171 = f32[3,2048,64]{1,2,0:T(8,128)} fusion(f32[3,512,2048]{2,1,0:T(8,128)} %copy-done, f32[3,512,2048]{2,1,0:T(8,128)} %fusion.170, f32[3,2048,64]{1,2,0:T(8,128)} %get-tuple-element.574, pred[]{:T(512)S(6)} %compare.3, bf16[3,2048,64]{1,2,0:T(8,128)(2,1)} %get-tuple-element.593, s32[]{:T(128)S(6)} %select_n.227), kind=kOutput, calls=%fused_computation.37.clone.1 | convolution fusion | flops 419171840 | bytes 53673988 | tf_op jit(solution)/shard_map/while/body/eval_jaxpr/pqk,pqd->pkd/dot_general | solution.py:266
  663.1 35.9 %all-to-all-done.3 = bf16[8,3,3,16384]{3,1,2,0:T(4,128)(2,1)S(1)} async-done(((bf16[8,3,3,16384]{3,1,2,0:T(4,128)(2,1)}), bf16[8,3,3,16384]{3,1,2,0:T(4,128)(2,1)S(1)}, u32[]{:S(2)}, u32[]{:S(2)}) %all-to-all-start.3) | async-done | bytes 2359328 | tf_op jit(solution)/shard_map/all_to_all | solution.py:280
  703.1 6.9 gather_fusion.4
  713.2 8.4 reshape.610
  721.6 6.5 copy.142
  748.6 5.6 stack.69
  755.9 31.1 %reduce-scatter.15.cloned.1.call-done = bf16[768,288]{0,1:T(8,128)(2,1)} async-done(((bf16[768,2304]{0,1:T(8,128)(2,1)}), bf16[768,288]{0,1:T(8,128)(2,1)}) %reduce-scatter.15.cloned.1.call-update) | async-done | bytes 442384 | tf_op jit(solution)/shard_map/reduce_scatter | solution.py:293
  789.1 6.3 fusion.74
  795.4 40.4 %all-reduce = (f32[768]{0:T(1024)}, f32[768]{0:T(1024)}, f32[768]{0:T(1024)}, f32[768]{0:T(1024)}, f32[9]{0:T(128)}) all-reduce(f32[768]{0:T(1024)S(1)} %get-tuple-element.307, f32[768]{0:T(1024)S(1)} %get-tuple-element.312, f32[768]{0:T(1024)S(1)} %copy-done.29, ...), channel_id=1, replica_groups=mesh['batch'=4,'seq'=8] {'batch','seq'}, use_global_device_ids=true, to_apply=%region_25.28 | all-reduce | flops 3081 | bytes 24648 | tf_op jit(solution)/shard_map/psum | solution.py:320
  842.0 15.0 %reduce-scatter.25.cloned.1.call-done = bf16[192,288]{1,0:T(8,128)(2,1)} async-done(((bf16[768,288]{1,0:T(8,128)(2,1)}), bf16[192,288]{1,0:T(8,128)(2,1)}) %reduce-scatter.25.cloned.1.call-update) | async-done | bytes 110608
  (315 shorter events, 252.1 us)
Async XLA Ops:
  7.2 34.5 %copy-start.18 = (bf16[192,384]{1,0:T(8,128)(2,1)S(1)}, bf16[192,384]{1,0:T(8,128)(2,1)}, u32[]{:S(2)}) copy-start(bf16[192,384]{1,0:T(8,128)(2,1)} %param.27) | copy-start | bytes 442372
  7.2 51.6 %copy-start.44 = (s32[1,2]{1,0:T(1,128)S(1)}, s32[1,2]{1,0:T(1,128)}, u32[]{:S(2)}) copy-start(s32[1,2]{1,0:T(1,128)} %param.35) | copy-start | bytes 28
  7.2 51.7 %copy-start.37 = (s32[1,24]{1,0:T(1,128)S(1)}, s32[1,24]{1,0:T(1,128)}, u32[]{:S(2)}) copy-start(s32[1,24]{1,0:T(1,128)} %param.34) | copy-start | bytes 292
  7.2 51.8 %copy-start.3 = (bf16[512,768]{1,0:T(8,128)(2,1)S(1)}, bf16[512,768]{1,0:T(8,128)(2,1)}, u32[]{:S(2)}) copy-start(bf16[512,768]{1,0:T(8,128)(2,1)} %param.22) | copy-start | bytes 2359300
  7.2 55.3 %all-gather.5.cloned.1.call-start = ((), (), s32[]{:S(2)}) async-start(), calls=%async_computation.12 | async-start | bytes 3981312 | tf_op jit(solution)/shard_map/all_gather | solution.py:143
  26.9 35.7 %copy-start.31 = (f32[768]{0:T(1024)S(1)}, f32[768]{0:T(1024)}, u32[]{:S(2)}) copy-start(f32[768]{0:T(1024)} %param.29) | copy-start | bytes 9220
  26.9 35.7 %copy-start.42 = (f32[768]{0:T(1024)S(1)}, f32[768]{0:T(1024)}, u32[]{:S(2)}) copy-start(f32[768]{0:T(1024)} %param.30) | copy-start | bytes 9220
  26.9 268.4 %all-gather.7.cloned.1.call-start = ((), (), s32[]{:S(2)}) async-start(), calls=%async_computation.13 | async-start | bytes 1327104 | tf_op jit(solution)/shard_map/all_gather | solution.py:144
  41.6 256.5 %all-gather.9.cloned.1.call-start = ((), (), s32[]{:S(2)}) async-start(), calls=%async_computation.14 | async-start | bytes 5308416 | tf_op jit(solution)/shard_map/all_gather | solution.py:145
  59.2 7.5 copy-start.22
  62.5 14.6 %copy-start.13 = (f32[2,256,32]{1,0,2:T(2,128)}, f32[2,256,32]{1,0,2:T(2,128)S(1)}, u32[]{:S(2)}) copy-start(f32[2,256,32]{1,0,2:T(2,128)S(1)} %get-tuple-element.381) | copy-start | bytes 196612
  62.5 14.6 %copy-start.15 = (f32[2,256,32]{1,0,2:T(2,128)}, f32[2,256,32]{1,0,2:T(2,128)S(1)}, u32[]{:S(2)}) copy-start(f32[2,256,32]{1,0,2:T(2,128)S(1)} %get-tuple-element.382) | copy-start | bytes 196612
  62.5 36.9 %copy-start.26 = (s32[1024]{0:T(1024)}, s32[1024]{0:T(1024)S(1)}, u32[]{:S(2)}) copy-start(s32[1024]{0:T(1024)S(1)} %get-tuple-element.404) | copy-start | bytes 12292
  62.5 44.1 %copy-start.33 = (pred[24]{0:T(512)(128)(4,1)}, pred[24]{0:T(512)(128)(4,1)S(1)}, u32[]{:S(2)}) copy-start(pred[24]{0:T(512)(128)(4,1)S(1)} %compare_and_fusion.1) | copy-start | bytes 76
  62.5 4.2 copy-start.24
  112.2 3.9 copy-start.19
  112.2 49.9 %all-to-all-start = ((bf16[8,3,3,16384]{3,1,2,0:T(4,128)(2,1)}), bf16[8,3,3,16384]{3,1,2,0:T(4,128)(2,1)S(1)}, u32[]{:S(2)}, u32[]{:S(2)}) async-start(bf16[8,3,3,16384]{3,1,2,0:T(4,128)(2,1)} %copy.121), calls=%async_computation | async-start | bytes 6291456 | tf_op jit(solution)/shard_map/all_to_all | solution.py:158
  116.0 189.2 %all-gather.11.cloned.1.call-start = ((), (), s32[]{:S(2)}) async-start(), calls=%async_computation.15 | async-start | bytes 5308416 | tf_op jit(solution)/shard_map/all_gather | solution.py:146
  267.0 5.3 copy-start.38
  267.0 6.0 copy-start.20
  268.7 18.9 %all-to-all-start.1 = ((bf16[8,3,1,16384]{3,1,2,0:T(4,128)(2,1)}), bf16[8,3,1,16384]{3,1,2,0:T(4,128)(2,1)S(1)}, u32[]{:S(2)}, u32[]{:S(2)}) async-start(bf16[8,3,1,16384]{3,1,2,0:T(4,128)(2,1)} %copy.127), calls=%async_computation.1 | async-start | bytes 2097152 | tf_op jit(solution)/shard_map/all_to_all | solution.py:193
  272.2 389.1 %reduce-scatter.17.cloned.1.call-start = ((), (), s32[]{:S(2)}) async-start(), calls=%async_computation.17 | async-start | bytes 1327104 | tf_op jit(solution)/shard_map/reduce_scatter | solution.py:296
  273.0 16.3 %copy-start.27 = (s32[1024]{0:T(1024)}, s32[1024]{0:T(1024)S(1)}, u32[]{:S(2)}) copy-start(s32[1024]{0:T(1024)S(1)} %pad_clamp_fusion) | copy-start | bytes 12292
  273.7 15.6 %copy-start.35 = (pred[24]{0:T(512)(128)(4,1)}, pred[24]{0:T(512)(128)(4,1)S(1)}, u32[]{:S(2)}) copy-start(pred[24]{0:T(512)(128)(4,1)S(1)} %compare_and_fusion) | copy-start | bytes 76
  291.1 4.2 copy-start.4
  298.0 7.2 copy-start.9
  305.2 10.1 %copy-start.39 = (bf16[768,3072]{1,0:T(8,128)(2,1)S(1)}, bf16[768,3072]{1,0:T(8,128)(2,1)}, u32[]{:S(2)}) copy-start(bf16[768,3072]{1,0:T(8,128)(2,1)} %all-gather.9.cloned.1.call-done) | copy-start | bytes 14155780
  318.9 15.2 %slice-start = ((s8[6291456]{0:T(1024)(128)(4,1)}), s8[4194304]{0:T(1024)(128)(4,1)S(1)}, s32[]{:S(2)}) async-start(s8[6291456]{0:T(1024)(128)(4,1)} %bitcast.246), calls=%async_computation.24 | async-start | bytes 8388608
  318.9 15.2 %slice-start.1 = ((s8[6291456]{0:T(1024)(128)(4,1)}), s8[2097152]{0:T(1024)(128)(4,1)S(1)}, s32[]{:S(2)}) async-start(s8[6291456]{0:T(1024)(128)(4,1)} %bitcast.246), calls=%async_computation.25 | async-start | bytes 4194304
  318.9 15.2 %copy-start.10 = (bf16[512,768]{1,0:T(8,128)(2,1)S(1)}, bf16[512,768]{1,0:T(8,128)(2,1)}, u32[]{:S(2)}) copy-start(bf16[512,768]{1,0:T(8,128)(2,1)} %param.24) | copy-start | bytes 2359300
  334.1 4.9 copy-start.6
  341.0 398.9 %reduce-scatter.29.cloned.1.call-start = ((), (), s32[]{:S(2)}) async-start(), calls=%async_computation.23 | async-start | bytes 5308416
  370.9 18.9 %all-to-all-start.2 = ((bf16[8,3,1,16384]{3,1,2,0:T(4,128)(2,1)}), bf16[8,3,1,16384]{3,1,2,0:T(4,128)(2,1)S(1)}, u32[]{:S(2)}, u32[]{:S(2)}) async-start(bf16[8,3,1,16384]{3,1,2,0:T(4,128)(2,1)} %bitcast.250), calls=%async_computation.2 | async-start | bytes 2097152 | tf_op jit(solution)/shard_map/all_to_all | solution.py:242
  374.5 367.8 %reduce-scatter.21.cloned.1.call-start = ((), (), s32[]{:S(2)}) async-start(), calls=%async_computation.19 | async-start | bytes 5308416 | tf_op jit(solution)/shard_map/reduce_scatter | solution.py:302
  406.8 4.5 copy-start
  468.4 4.5 copy-start
  528.0 4.5 copy-start
  587.0 4.5 copy-start
  657.6 41.4 %all-to-all-start.3 = ((bf16[8,3,3,16384]{3,1,2,0:T(4,128)(2,1)}), bf16[8,3,3,16384]{3,1,2,0:T(4,128)(2,1)S(1)}, u32[]{:S(2)}, u32[]{:S(2)}) async-start(bf16[8,3,3,16384]{3,1,2,0:T(4,128)(2,1)} %copy.138), calls=%async_computation.3 | async-start | bytes 6291456 | tf_op jit(solution)/shard_map/all_to_all | solution.py:280
  661.2 93.0 %reduce-scatter.27.cloned.1.call-start = ((), (), s32[]{:S(2)}) async-start(), calls=%async_computation.22 | async-start | bytes 245760
  663.1 123.9 %reduce-scatter.15.cloned.1.call-start = ((), (), s32[]{:S(2)}) async-start(), calls=%async_computation.16 | async-start | bytes 3981312 | tf_op jit(solution)/shard_map/reduce_scatter | solution.py:293
  703.1 7.0 copy-start.36
  739.9 98.8 %reduce-scatter.19.cloned.1.call-start = ((), (), s32[]{:S(2)}) async-start(), calls=%async_computation.18 | async-start | bytes 737280 | tf_op jit(solution)/shard_map/reduce_scatter | solution.py:313
  742.2 98.2 %reduce-scatter.23.cloned.1.call-start = ((), (), s32[]{:S(2)}) async-start(), calls=%async_computation.20 | async-start | bytes 737280 | tf_op jit(solution)/shard_map/reduce_scatter | solution.py:316
  742.9 114.1 %reduce-scatter.25.cloned.1.call-start = ((), (), s32[]{:S(2)}) async-start(), calls=%async_computation.21 | async-start | bytes 737280
  789.1 6.4 copy-start.29
  789.1 6.4 copy-start.30
  789.1 46.8 %copy-start.2 = (f32[512,768]{1,0:T(8,128)S(1)}, f32[512,768]{1,0:T(8,128)}, u32[]{:S(2)}) copy-start(f32[512,768]{1,0:T(8,128)} %copy-done.1) | copy-start | bytes 4718596
  (19 other events, 43.1 us)
Sparse Core Ops, SparseCore 0:
  27.0 35.0 all-gather.4
  64.5 23.9 all-gather.6
  90.4 47.8 all-gather.8
  139.9 55.3 all-gather.10
  341.1 35.5 reduce-scatter.16
  380.0 53.7 reduce-scatter.28
  437.3 53.7 reduce-scatter.20
  664.9 20.7 reduce-scatter.26
  740.0 46.9 reduce-scatter.14
  789.1 22.1 reduce-scatter.18
  813.6 20.6 reduce-scatter.22
  836.4 20.6 reduce-scatter.24
where the time goes:
time: 872 us; the launch traced here: 866 us
  matrix products  330 us (38%)
  local copies, waits for them, and re-layouts  179 us (21%)
  waiting for transfers between devices  131 us (15%)
  blocking collectives  107 us (12%)
  other arithmetic  71.9 us (8%)
  loops' own time  16.5 us (2%)
  between operations  15.6 us (2%)
  starting transfers between devices  15.3 us (2%)
    dot_general x4, matrix products, backward_block(): jnp.einsum('pqk,pqd->pkd', dscore, query_block, preferred_element_type=jn...  82.2 us
    dot_general x4, matrix products, backward_block(): jnp.einsum('pqk,pkd->pqd', dscore, key_pairs, preferred_element_type=jnp....  72.8 us
    dot_general x8, matrix products, masked_scores(): jnp.einsum('pqd,pkd->pqk', query_block, key_pairs, preferred_element_type...  46.4 us
    psum x1, blocking collectives, local(): lax.psum((gain1_local, bias1_local, gain2_local, bias2_local, dwa_local),...  40.4 us
    all_to_all x1, waiting for transfers between devices, local(): lax.all_to_all(pairs_split(dpairs, n_seq), 'seq', split_axis=0, concat_ax...  35.9 us
    reduce_scatter x1, waiting for transfers between devices, local(): lax.psum_scatter(qkv_local.astype(jnp.bfloat16), 'seq', scatter_dimension...  31.1 us
    unnamed x112, local copies, waits for them, and re-layouts  29.7 us
    all_to_all x1, waiting for transfers between devices, local(): lax.all_to_all(to_pairs(stacked, order_row, n_seq, per_dev), 'seq', split...  27.8 us
  transfers between devices with their start and end apart: 16, of which 6 were waited for; matrix products, arithmetic and copies ran while one was open for 61% of the time, Pallas kernels for 0%

commit v1 on v0

--- a/solution.py
+++ b/solution.py
@@ -10,6 +10,28 @@
 HIST = 8
 NORM_EPS = 1e-05
 MASKED = -1e30
+
+
+def cut_along(x, dim, peers):
+    before, after = (x.shape[:dim], x.shape[dim + 1 :])
+    return jnp.moveaxis(x.reshape(*before, peers, -1, *after), dim, 0)
+
+
+def laid_out(tiles, dim):
+    shape = list(tiles.shape[1:])
+    shape[dim] *= tiles.shape[0]
+    return jnp.moveaxis(tiles, 0, dim).reshape(shape)
+
+
+def pairwise_exchange(x, axis, split_dim, concat_dim):
+    size, mine = (lax.axis_size(axis), lax.axis_index(axis))
+    parts = cut_along(x, split_dim, size)
+    outs = [parts[mine]]
+    for step in range(1, size):
+        sent = parts[mine ^ step]
+        outs.append(lax.ppermute(sent, axis, [(i, i ^ step) for i in range(size)]))
+    parts = jnp.stack(outs)[mine ^ jnp.arange(size)]
+    return laid_out(parts, concat_dim)
 
 
 def norm_rows(values, gain, shift):
@@ -277,9 +299,7 @@
     )
     dquery = jnp.transpose(dquery_blocks, (1, 0, 2, 3)).reshape(per_dev, SLOT, HD)
     dpairs = jnp.stack([dquery, dkeys_sum, dvalues_sum], axis=1).astype(jnp.bfloat16)
-    dreturned = lax.all_to_all(
-        pairs_split(dpairs, n_seq), "seq", split_axis=0, concat_axis=0, tiled=True
-    )
+    dreturned = pairwise_exchange(pairs_split(dpairs, n_seq), "seq", 0, 0)
     dtokens = tokens_back(dreturned, inverse, slot_count, HD)
     dq_rows = unrotate(dtokens[:, :, 0].astype(jnp.float32), cosine, sine_tab).reshape(row_count, D)
     dk_rows = unrotate(dtokens[:, :, 1].astype(jnp.float32), cosine, sine_tab).reshape(row_count, D)

time: 872 us -> 982 us (1.13)
  waiting for transfers between devices: 131 us -> 241 us
    reduce_scatter x1, waiting for transfers between devices: 0.02 us -> 44.2 us  [local(): lax.psum_scatter(down_local.astype(jnp.bfloat16), 'seq', scatter_dimensio...]
    unnamed x15, waiting for transfers between devices: 15.9 us -> 55.3 us
    all_to_all x1 -> x0, waiting for transfers between devices: 35.9 us -> none  [local(): lax.all_to_all(pairs_split(dpairs, n_seq), 'seq', split_axis=0, concat_ax...]
    ppermute x0 -> x7, waiting for transfers between devices: none -> 31.7 us  [pairwise_exchange(): outs.append(lax.ppermute(sent, axis, [(i, i ^ step) for i in range(size)]))]
    reduce_scatter x1, waiting for transfers between devices: 0.01 us -> 21.2 us  [local(): lax.psum_scatter(col_sums[3].astype(jnp.bfloat16), 'batch', scatter_dimen...]
    reduce_scatter x1, waiting for transfers between devices: 0.01 us -> 15 us  [local(): lax.psum_scatter(col_sums[2].astype(jnp.bfloat16), 'batch', scatter_dimen...]
    reduce_scatter x1, waiting for transfers between devices: 31.1 us -> 20.8 us  [local(): lax.psum_scatter(qkv_local.astype(jnp.bfloat16), 'seq', scatter_dimension...]
    unnamed x112 -> x139, local copies, waits for them, and re-layouts: 29.7 us -> 35.9 us
  transfers between devices with their start and end apart: 16 -> 22, of which waited for: 6 -> 11; matrix products, arithmetic and copies ran while one was open for 61% -> 53% of each run, Pallas kernels for 0% -> 0%
where the time goes in v1:
time: 982 us; the launch traced here: 977 us
  matrix products  325 us (33%)
  waiting for transfers between devices  241 us (25%)
  local copies, waits for them, and re-layouts  184 us (19%)
  blocking collectives  107 us (11%)
  other arithmetic  70.7 us (7%)
  loops' own time  16.7 us (2%)
  starting transfers between devices  16 us (2%)
  between operations  15.9 us (2%)
    dot_general x4, matrix products, backward_block(): jnp.einsum('pqk,pqd->pkd', dscore, query_block, preferred_element_type=jn...  79.8 us
    dot_general x4, matrix products, backward_block(): jnp.einsum('pqk,pkd->pqd', dscore, key_pairs, preferred_element_type=jnp....  71.7 us
    unnamed x15, waiting for transfers between devices  55.3 us
    dot_general x8, matrix products, masked_scores(): jnp.einsum('pqd,pkd->pqk', query_block, key_pairs, preferred_element_type...  46.4 us
    reduce_scatter x1, waiting for transfers between devices, local(): lax.psum_scatter(down_local.astype(jnp.bfloat16), 'seq', scatter_dimensio...  44.2 us
    psum x1, blocking collectives, local(): lax.psum((gain1_local, bias1_local, gain2_local, bias2_local, dwa_local),...  40.4 us
    unnamed x139, local copies, waits for them, and re-layouts  35.9 us
    ppermute x7, waiting for transfers between devices, pairwise_exchange(): outs.append(lax.ppermute(sent, axis, [(i, i ^ step) for i in range(size)]))  31.7 us
  transfers between devices with their start and end apart: 22, of which 11 were waited for; matrix products, arithmetic and copies ran while one was open for 53% of the time, Pallas kernels for 0%

profile of v1, /device:TPU:0, one launch (start us, length us, event | category | flops | bytes accessed | tf_op | source)
XLA Modules:
  0.0 976.5 jit_solution(8724100538782581522)
XLA Ops:
  7.3 18.6 %all_gather.32 = bf16[768,288]{1,0:T(8,128)(2,1)S(1)} all-gather(bf16[192,288]{1,0:T(8,128)(2,1)} %param.25), channel_id=1, replica_groups=mesh['batch'=4,'seq'=8] {'batch'}, dimensions={0}, use_global_device_ids=true | all-gather | bytes 552960 | tf_op jit(solution)/shard_map/all_gather | solution.py:159
  27.0 13.8 %all_gather.34 = bf16[768,96]{1,0:T(8,128)(2,1)S(1)} all-gather(bf16[192,96]{1,0:T(8,128)(2,1)} %param.26), channel_id=1, replica_groups=mesh['batch'=4,'seq'=8] {'batch'}, dimensions={0}, use_global_device_ids=true | all-gather | bytes 184320 | tf_op jit(solution)/shard_map/all_gather | solution.py:160
  41.7 17.0 %all_gather.36 = bf16[768,384]{1,0:T(8,128)(2,1)} all-gather(bf16[192,384]{1,0:T(8,128)(2,1)S(1)} %copy-done.20), channel_id=1, replica_groups=mesh['batch'=4,'seq'=8] {'batch'}, dimensions={0}, use_global_device_ids=true | all-gather | bytes 737280 | tf_op jit(solution)/shard_map/all_gather | solution.py:161
  91.2 8.1 reshape.655
  99.4 7.2 gather_fusion.2
  116.1 17.4 %all_gather.38 = bf16[3072,96]{0,1:T(8,128)(2,1)} all-gather(bf16[768,96]{0,1:T(8,128)(2,1)S(1)} %copy-done.21), channel_id=1, replica_groups=mesh['batch'=4,'seq'=8] {'batch'}, dimensions={0}, use_global_device_ids=true | all-gather | bytes 737280 | tf_op jit(solution)/shard_map/all_gather | solution.py:162
  134.2 27.8 %all-to-all-done = bf16[8,3,3,16384]{3,1,2,0:T(4,128)(2,1)S(1)} async-done(((bf16[8,3,3,16384]{3,1,2,0:T(4,128)(2,1)}), bf16[8,3,3,16384]{3,1,2,0:T(4,128)(2,1)S(1)}, u32[]{:S(2)}, u32[]{:S(2)}) %all-to-all-start) | async-done | bytes 2359328 | tf_op jit(solution)/shard_map/all_to_all | solution.py:180
  165.2 7.1 reshape.553
  181.9 80.9 %while.28 = (s32[]{:T(128)}, bf16[4,3,512,64]{2,3,1,0:T(8,128)(2,1)}, f32[4,3,512]{2,1,0:T(4,128)S(1)}, s32[4]{0:T(128)S(1)}, s32[3,2048]{1,0:T(4,128)S(1)}, /*i...) while((s32[]{:T(128)}, ...), condition=%wide.region_5.7_spmd.clone, body=%wide.region_2.6_spmd.clone.sunk | while | flops 863075328 | bytes 44073140 | solution.py:212
  256.9 5.8 fusion.160
  273.4 13.9 %all-to-all-done.1 = bf16[8,3,1,16384]{3,1,2,0:T(4,128)(2,1)S(1)} async-done(((bf16[8,3,1,16384]{3,1,2,0:T(4,128)(2,1)}), bf16[8,3,1,16384]{3,1,2,0:T(4,128)(2,1)S(1)}, u32[]{:S(2)}, u32[]{:S(2)}) %all-to-all-start.1) | async-done | bytes 786464 | tf_op jit(solution)/shard_map/all_to_all | solution.py:215
  297.9 7.3 fusion.112
  305.2 10.1 %fusion.58 = bf16[512,3072]{1,0:T(8,128)(2,1)S(1)} fusion(f32[512,3072]{1,0:T(8,128)} %fusion.112, bf16[3072,768]{0,1:T(8,128)(2,1)} %all-gather.11.cloned.1.call-done, bf16[512,768]{1,0:T(8,128)(2,1)S(1)} %copy-done.12, f32[]{:T(128)} %bitcast), kind=kOutput, calls=%fused_computation.66 | convolution fusion | flops 2448556032 | bytes 14942212 | tf_op jit(solution)/shard_map/nd,fd->nf/dot_general | solution.py:252
  318.8 14.8 %fusion.84 = (bf16[512,768]{1,0:T(8,128)(2,1)}, f32[512,768]{1,0:T(8,128)S(1)}) fusion(f32[]{:T(128)} %bitcast.39, f32[]{:T(128)} %bitcast.37, f32[]{:T(128)} %bitcast.35, f32[]{:T(128)} %bitcast.33, f32[]{:T(128)} %bitcast.31, f32[]{:T(128)} %bitcast.29, f32[]{:T(128)} %bitcast.27, f32[]{:T(128)} %bitcast.25, f32[]{:T(128)} %bitcast, ...), kind=kOutput, calls=%fused_computation.120 | convolution fusion | flops 2440691712 | bytes 21233700 | tf_op jit(solution)/shard_map/dot_general | solution.py:225
  355.5 10.9 %all-to-all-done.2 = bf16[8,3,1,16384]{3,1,2,0:T(4,128)(2,1)S(1)} async-done(((bf16[8,3,1,16384]{3,1,2,0:T(4,128)(2,1)}), bf16[8,3,1,16384]{3,1,2,0:T(4,128)(2,1)S(1)}, u32[]{:S(2)}, u32[]{:S(2)}) %all-to-all-start.2) | async-done | bytes 786464 | tf_op jit(solution)/shard_map/all_to_all | solution.py:264
  373.0 237.2 %while.29 = (s32[]{:T(128)}, f32[3,2048,64]{1,2,0:T(8,128)}, f32[3,2048,64]{1,2,0:T(8,128)S(1)}, bf16[4,3,512,64]{2,3,1,0:T(8,128)(2,1)}, s32[4]{0:T(128)S(1)}, ...) while((s32[]{:T(128)}, f32[3,2048,64]{1,2,0:T(8,128)}, ...), condition=%wide.region_13.16_spmd.clone, body=%wide.region_11.15_spmd.clone.sunk | while | flops 2066226688 | bytes 200737024 | solution.py:297
  377.4 6.1 subtract_exponential_fusion.3
  388.1 6.4 fusion.171
  394.5 17.9 %fusion.174 = bf16[4,3,512,64]{2,3,1,0:T(8,128)(2,1)} fusion(bf16[4,3,512,64]{2,3,1,0:T(8,128)(2,1)} %get-tuple-element.584, s32[]{:T(128)S(6)} %copy.219, bf16[3,2048,64]{1,2,0:T(8,128)(2,1)} %get-tuple-element.602, f32[3,512,2048]{2,1,0:T(8,128)} %copy-done, f32[3,512,2048]{2,1,0:T(8,128)} %fusion.171), kind=kOutput, calls=%fused_computation.40.clone.1 | convolution fusion | flops 418385408 | bytes 51511300 | tf_op jit(solution)/shard_map/while/body/eval_jaxpr/pqk,pkd->pqd/dot_general | solution.py:285
  412.4 19.6 %fusion.172 = f32[3,2048,64]{1,2,0:T(8,128)} fusion(f32[3,512,2048]{2,1,0:T(8,128)} %copy-done, f32[3,512,2048]{2,1,0:T(8,128)} %fusion.171, f32[3,2048,64]{1,2,0:T(8,128)} %get-tuple-element.582, pred[]{:T(512)S(6)} %compare.3, bf16[3,2048,64]{1,2,0:T(8,128)(2,1)} %get-tuple-element.601, s32[]{:T(128)S(6)} %select_n.273), kind=kOutput, calls=%fused_computation.38.clone.1 | convolution fusion | flops 419171840 | bytes 53673988 | tf_op jit(solution)/shard_map/while/body/eval_jaxpr/pqk,pqd->pkd/dot_general | solution.py:288
  436.3 6.1 subtract_exponential_fusion.3
  446.9 6.4 fusion.171
  453.4 17.9 %fusion.174 = bf16[4,3,512,64]{2,3,1,0:T(8,128)(2,1)} fusion(bf16[4,3,512,64]{2,3,1,0:T(8,128)(2,1)} %get-tuple-element.584, s32[]{:T(128)S(6)} %copy.219, bf16[3,2048,64]{1,2,0:T(8,128)(2,1)} %get-tuple-element.602, f32[3,512,2048]{2,1,0:T(8,128)} %copy-done, f32[3,512,2048]{2,1,0:T(8,128)} %fusion.171), kind=kOutput, calls=%fused_computation.40.clone.1 | convolution fusion | flops 418385408 | bytes 51511300 | tf_op jit(solution)/shard_map/while/body/eval_jaxpr/pqk,pkd->pqd/dot_general | solution.py:285
  471.3 20.1 %fusion.172 = f32[3,2048,64]{1,2,0:T(8,128)} fusion(f32[3,512,2048]{2,1,0:T(8,128)} %copy-done, f32[3,512,2048]{2,1,0:T(8,128)} %fusion.171, f32[3,2048,64]{1,2,0:T(8,128)} %get-tuple-element.582, pred[]{:T(512)S(6)} %compare.3, bf16[3,2048,64]{1,2,0:T(8,128)(2,1)} %get-tuple-element.601, s32[]{:T(128)S(6)} %select_n.273), kind=kOutput, calls=%fused_computation.38.clone.1 | convolution fusion | flops 419171840 | bytes 53673988 | tf_op jit(solution)/shard_map/while/body/eval_jaxpr/pqk,pqd->pkd/dot_general | solution.py:288
  495.6 6.1 subtract_exponential_fusion.3
  506.3 6.4 fusion.171
  512.7 17.9 %fusion.174 = bf16[4,3,512,64]{2,3,1,0:T(8,128)(2,1)} fusion(bf16[4,3,512,64]{2,3,1,0:T(8,128)(2,1)} %get-tuple-element.584, s32[]{:T(128)S(6)} %copy.219, bf16[3,2048,64]{1,2,0:T(8,128)(2,1)} %get-tuple-element.602, f32[3,512,2048]{2,1,0:T(8,128)} %copy-done, f32[3,512,2048]{2,1,0:T(8,128)} %fusion.171), kind=kOutput, calls=%fused_computation.40.clone.1 | convolution fusion | flops 418385408 | bytes 51511300 | tf_op jit(solution)/shard_map/while/body/eval_jaxpr/pqk,pkd->pqd/dot_general | solution.py:285
  530.6 20.1 %fusion.172 = f32[3,2048,64]{1,2,0:T(8,128)} fusion(f32[3,512,2048]{2,1,0:T(8,128)} %copy-done, f32[3,512,2048]{2,1,0:T(8,128)} %fusion.171, f32[3,2048,64]{1,2,0:T(8,128)} %get-tuple-element.582, pred[]{:T(512)S(6)} %compare.3, bf16[3,2048,64]{1,2,0:T(8,128)(2,1)} %get-tuple-element.601, s32[]{:T(128)S(6)} %select_n.273), kind=kOutput, calls=%fused_computation.38.clone.1 | convolution fusion | flops 419171840 | bytes 53673988 | tf_op jit(solution)/shard_map/while/body/eval_jaxpr/pqk,pqd->pkd/dot_general | solution.py:288
  555.0 6.1 subtract_exponential_fusion.3
  565.6 6.4 fusion.171
  572.0 17.9 %fusion.174 = bf16[4,3,512,64]{2,3,1,0:T(8,128)(2,1)} fusion(bf16[4,3,512,64]{2,3,1,0:T(8,128)(2,1)} %get-tuple-element.584, s32[]{:T(128)S(6)} %copy.219, bf16[3,2048,64]{1,2,0:T(8,128)(2,1)} %get-tuple-element.602, f32[3,512,2048]{2,1,0:T(8,128)} %copy-done, f32[3,512,2048]{2,1,0:T(8,128)} %fusion.171), kind=kOutput, calls=%fused_computation.40.clone.1 | convolution fusion | flops 418385408 | bytes 51511300 | tf_op jit(solution)/shard_map/while/body/eval_jaxpr/pqk,pkd->pqd/dot_general | solution.py:285
  590.0 20.1 %fusion.172 = f32[3,2048,64]{1,2,0:T(8,128)} fusion(f32[3,512,2048]{2,1,0:T(8,128)} %copy-done, f32[3,512,2048]{2,1,0:T(8,128)} %fusion.171, f32[3,2048,64]{1,2,0:T(8,128)} %get-tuple-element.582, pred[]{:T(512)S(6)} %compare.3, bf16[3,2048,64]{1,2,0:T(8,128)(2,1)} %get-tuple-element.601, s32[]{:T(128)S(6)} %select_n.273), kind=kOutput, calls=%fused_computation.38.clone.1 | convolution fusion | flops 419171840 | bytes 53673988 | tf_op jit(solution)/shard_map/while/body/eval_jaxpr/pqk,pqd->pkd/dot_general | solution.py:288
  627.6 6.4 constant_dynamic-slice_fusion.3
  641.9 6.4 collective-permute-done.1
  648.4 7.2 collective-permute-done.2
  656.0 18.1 %collective-permute-done.4 = bf16[1,3,3,16384]{3,2,1,0:T(4,128)(2,1)S(1)} collective-permute-done((bf16[1,3,3,16384]{3,2,1,0:T(4,128)(2,1)S(1)}, bf16[1,3,3,16384]{3,2,1,0:T(4,128)(2,1)S(1)}, u32[]{:S(2)}, u32[]{:S(2)}) %collective-permute-start.4) | collective-permute-done | bytes 294944 | tf_op jit(solution)/shard_map/ppermute | solution.py:32
  690.5 6.3 reshape.658
  696.8 6.5 copy.165
  716.6 6.5 convolution_convert_fusion.2
  723.1 6.8 copy.178
  731.0 8.6 convolution_convert_fusion.1
  741.6 20.8 %reduce-scatter.15.cloned.1.call-done = bf16[768,288]{0,1:T(8,128)(2,1)} async-done(((bf16[768,2304]{0,1:T(8,128)(2,1)}), bf16[768,288]{0,1:T(8,128)(2,1)}) %reduce-scatter.15.cloned.1.call-update) | async-done | bytes 442384 | tf_op jit(solution)/shard_map/reduce_scatter | solution.py:313
  764.5 55.1 %reduce-scatter.29.cloned.1.call-done = bf16[384,768]{1,0:T(8,128)(2,1)} async-done(((bf16[3072,768]{1,0:T(8,128)(2,1)}), bf16[384,768]{1,0:T(8,128)(2,1)}) %reduce-scatter.29.cloned.1.call-update) | async-done | bytes 589840
  832.7 44.2 %reduce-scatter.21.cloned.1.call-done = bf16[3072,96]{0,1:T(8,128)(2,1)} async-done(((bf16[3072,768]{0,1:T(8,128)(2,1)}), bf16[3072,96]{0,1:T(8,128)(2,1)}) %reduce-scatter.21.cloned.1.call-update) | async-done | bytes 589840 | tf_op jit(solution)/shard_map/reduce_scatter | solution.py:322
  876.9 6.4 fusion.74
  883.3 40.4 %all-reduce = (f32[768]{0:T(1024)}, f32[768]{0:T(1024)}, f32[768]{0:T(1024)}, f32[768]{0:T(1024)}, f32[9]{0:T(128)}) all-reduce(f32[768]{0:T(1024)S(1)} %get-tuple-element.307, f32[768]{0:T(1024)S(1)} %get-tuple-element.312, f32[768]{0:T(1024)S(1)} %copy-done.36, ...), channel_id=1, replica_groups=mesh['batch'=4,'seq'=8] {'batch','seq'}, use_global_device_ids=true, to_apply=%region_25.28 | all-reduce | flops 3081 | bytes 24648 | tf_op jit(solution)/shard_map/psum | solution.py:340
  930.0 15.0 %reduce-scatter.19.cloned.1.call-done = bf16[192,384]{1,0:T(8,128)(2,1)} async-done(((bf16[768,384]{1,0:T(8,128)(2,1)}), bf16[192,384]{1,0:T(8,128)(2,1)}) %reduce-scatter.19.cloned.1.call-update) | async-done | bytes 147472 | tf_op jit(solution)/shard_map/reduce_scatter | solution.py:333
  946.6 21.2 %reduce-scatter.23.cloned.1.call-done = bf16[768,96]{0,1:T(8,128)(2,1)} async-done(((bf16[3072,96]{0,1:T(8,128)(2,1)}), bf16[768,96]{0,1:T(8,128)(2,1)}) %reduce-scatter.23.cloned.1.call-update) | async-done | bytes 147472 | tf_op jit(solution)/shard_map/reduce_scatter | solution.py:336
  (364 shorter events, 286.4 us)
Async XLA Ops:
  7.2 34.5 %copy-start.20 = (bf16[192,384]{1,0:T(8,128)(2,1)S(1)}, bf16[192,384]{1,0:T(8,128)(2,1)}, u32[]{:S(2)}) copy-start(bf16[192,384]{1,0:T(8,128)(2,1)} %param.27) | copy-start | bytes 442372
  7.2 51.6 %copy-start.53 = (s32[1,2]{1,0:T(1,128)S(1)}, s32[1,2]{1,0:T(1,128)}, u32[]{:S(2)}) copy-start(s32[1,2]{1,0:T(1,128)} %param.35) | copy-start | bytes 28
  7.2 51.7 %copy-start.44 = (s32[1,24]{1,0:T(1,128)S(1)}, s32[1,24]{1,0:T(1,128)}, u32[]{:S(2)}) copy-start(s32[1,24]{1,0:T(1,128)} %param.34) | copy-start | bytes 292
  7.2 51.8 %copy-start.3 = (bf16[512,768]{1,0:T(8,128)(2,1)S(1)}, bf16[512,768]{1,0:T(8,128)(2,1)}, u32[]{:S(2)}) copy-start(bf16[512,768]{1,0:T(8,128)(2,1)} %param.22) | copy-start | bytes 2359300
  7.2 55.3 %all-gather.5.cloned.1.call-start = ((), (), s32[]{:S(2)}) async-start(), calls=%async_computation.11 | async-start | bytes 3981312 | tf_op jit(solution)/shard_map/all_gather | solution.py:165
  26.9 35.7 %copy-start.38 = (f32[768]{0:T(1024)S(1)}, f32[768]{0:T(1024)}, u32[]{:S(2)}) copy-start(f32[768]{0:T(1024)} %param.29) | copy-start | bytes 9220
  26.9 35.7 %copy-start.49 = (f32[768]{0:T(1024)S(1)}, f32[768]{0:T(1024)}, u32[]{:S(2)}) copy-start(f32[768]{0:T(1024)} %param.30) | copy-start | bytes 9220
  26.9 268.1 %all-gather.7.cloned.1.call-start = ((), (), s32[]{:S(2)}) async-start(), calls=%async_computation.12 | async-start | bytes 1327104 | tf_op jit(solution)/shard_map/all_gather | solution.py:166
  41.6 256.2 %all-gather.9.cloned.1.call-start = ((), (), s32[]{:S(2)}) async-start(), calls=%async_computation.13 | async-start | bytes 5308416 | tf_op jit(solution)/shard_map/all_gather | solution.py:167
  59.2 7.5 copy-start.24
  62.5 14.6 %copy-start.15 = (f32[2,256,32]{1,0,2:T(2,128)}, f32[2,256,32]{1,0,2:T(2,128)S(1)}, u32[]{:S(2)}) copy-start(f32[2,256,32]{1,0,2:T(2,128)S(1)} %get-tuple-element.389) | copy-start | bytes 196612
  62.5 14.6 %copy-start.17 = (f32[2,256,32]{1,0,2:T(2,128)}, f32[2,256,32]{1,0,2:T(2,128)S(1)}, u32[]{:S(2)}) copy-start(f32[2,256,32]{1,0,2:T(2,128)S(1)} %get-tuple-element.390) | copy-start | bytes 196612
  62.5 36.9 %copy-start.33 = (s32[1024]{0:T(1024)}, s32[1024]{0:T(1024)S(1)}, u32[]{:S(2)}) copy-start(s32[1024]{0:T(1024)S(1)} %get-tuple-element.412) | copy-start | bytes 12292
  62.5 44.1 %copy-start.42 = (pred[24]{0:T(512)(128)(4,1)}, pred[24]{0:T(512)(128)(4,1)S(1)}, u32[]{:S(2)}) copy-start(pred[24]{0:T(512)(128)(4,1)S(1)} %compare_and_fusion.1) | copy-start | bytes 76
  112.1 49.9 %all-to-all-start = ((bf16[8,3,3,16384]{3,1,2,0:T(4,128)(2,1)}), bf16[8,3,3,16384]{3,1,2,0:T(4,128)(2,1)S(1)}, u32[]{:S(2)}, u32[]{:S(2)}) async-start(bf16[8,3,3,16384]{3,1,2,0:T(4,128)(2,1)} %copy.139), calls=%async_computation | async-start | bytes 6291456 | tf_op jit(solution)/shard_map/all_to_all | solution.py:180
  116.0 189.1 %all-gather.11.cloned.1.call-start = ((), (), s32[]{:S(2)}) async-start(), calls=%async_computation.14 | async-start | bytes 5308416 | tf_op jit(solution)/shard_map/all_gather | solution.py:168
  266.8 5.9 copy-start.22
  268.4 18.9 %all-to-all-start.1 = ((bf16[8,3,1,16384]{3,1,2,0:T(4,128)(2,1)}), bf16[8,3,1,16384]{3,1,2,0:T(4,128)(2,1)S(1)}, u32[]{:S(2)}, u32[]{:S(2)}) async-start(bf16[8,3,1,16384]{3,1,2,0:T(4,128)(2,1)} %copy.145), calls=%async_computation.1 | async-start | bytes 2097152 | tf_op jit(solution)/shard_map/all_to_all | solution.py:215
  272.7 16.3 %copy-start.32 = (s32[1024]{0:T(1024)}, s32[1024]{0:T(1024)S(1)}, u32[]{:S(2)}) copy-start(s32[1024]{0:T(1024)S(1)} %pad_clamp_fusion.1) | copy-start | bytes 12292
  273.4 15.6 %copy-start.40 = (pred[24]{0:T(512)(128)(4,1)}, pred[24]{0:T(512)(128)(4,1)S(1)}, u32[]{:S(2)}) copy-start(pred[24]{0:T(512)(128)(4,1)S(1)} %compare_and_fusion) | copy-start | bytes 76
  297.4 36.2 %copy-start.6 = (f32[512,768]{1,0:T(8,128)}, f32[512,768]{1,0:T(8,128)S(1)}, u32[]{:S(2)}) copy-start(f32[512,768]{1,0:T(8,128)S(1)} %get-tuple-element.405) | copy-start | bytes 4718596
  297.5 36.2 %copy-start.26 = (f32[512]{0:T(512)}, f32[512]{0:T(512)S(1)}, u32[]{:S(2)}) copy-start(f32[512]{0:T(512)S(1)} %broadcast_multiply_fusion.5) | copy-start | bytes 6148
  297.8 35.9 %copy-start.30 = (f32[512]{0:T(512)}, f32[512]{0:T(512)S(1)}, u32[]{:S(2)}) copy-start(f32[512]{0:T(512)S(1)} %add_rsqrt_fusion) | copy-start | bytes 6148
  297.8 7.4 copy-start.12
  305.2 10.1 %copy-start.46 = (bf16[768,3072]{1,0:T(8,128)(2,1)S(1)}, bf16[768,3072]{1,0:T(8,128)(2,1)}, u32[]{:S(2)}) copy-start(bf16[768,3072]{1,0:T(8,128)(2,1)} %all-gather.9.cloned.1.call-done) | copy-start | bytes 14155780
  318.8 14.9 %slice-start = ((s8[6291456]{0:T(1024)(128)(4,1)}), s8[4194304]{0:T(1024)(128)(4,1)S(1)}, s32[]{:S(2)}) async-start(s8[6291456]{0:T(1024)(128)(4,1)} %bitcast.284), calls=%async_computation.23 | async-start | bytes 8388608
  318.8 14.9 %slice-start.1 = ((s8[6291456]{0:T(1024)(128)(4,1)}), s8[2097152]{0:T(1024)(128)(4,1)S(1)}, s32[]{:S(2)}) async-start(s8[6291456]{0:T(1024)(128)(4,1)} %bitcast.284), calls=%async_computation.24 | async-start | bytes 4194304
  347.5 18.9 %all-to-all-start.2 = ((bf16[8,3,1,16384]{3,1,2,0:T(4,128)(2,1)}), bf16[8,3,1,16384]{3,1,2,0:T(4,128)(2,1)S(1)}, u32[]{:S(2)}, u32[]{:S(2)}) async-start(bf16[8,3,1,16384]{3,1,2,0:T(4,128)(2,1)} %bitcast.45), calls=%async_computation.2 | async-start | bytes 2097152 | tf_op jit(solution)/shard_map/all_to_all | solution.py:264
  351.1 388.7 %reduce-scatter.17.cloned.1.call-start = ((), (), s32[]{:S(2)}) async-start(), calls=%async_computation.16 | async-start | bytes 1327104 | tf_op jit(solution)/shard_map/reduce_scatter | solution.py:316
  355.5 406.9 %reduce-scatter.15.cloned.1.call-start = ((), (), s32[]{:S(2)}) async-start(), calls=%async_computation.15 | async-start | bytes 3981312 | tf_op jit(solution)/shard_map/reduce_scatter | solution.py:313
  636.1 4.9 collective-permute-start
  636.2 12.1 %collective-permute-start.1 = (bf16[1,3,3,16384]{3,2,1,0:T(4,128)(2,1)S(1)}, bf16[1,3,3,16384]{3,2,1,0:T(4,128)(2,1)S(1)}, u32[]{:S(2)}, u32[]{:S(2)}) collective-permute-start(bf16[1,3,3,16384]{3,2,1,0:T(4,128)(2,1)S(1)} %bitcast.310), channel_id=1, source_target_pairs={{0,2},{1,3},{2,0},{3,1},{4,6},{5,7},{6,4},{7,5},{8,10},{9,11},{10,... | collective-permute-start | bytes 884744 | tf_op jit(solution)/shard_map/ppermute | solution.py:32
  636.9 18.7 %collective-permute-start.2 = (bf16[1,3,3,16384]{3,2,1,0:T(4,128)(2,1)S(1)}, bf16[1,3,3,16384]{3,2,1,0:T(4,128)(2,1)S(1)}, u32[]{:S(2)}, u32[]{:S(2)}) collective-permute-start(bf16[1,3,3,16384]{3,2,1,0:T(4,128)(2,1)S(1)} %bitcast.307), channel_id=1, source_target_pairs={{0,3},{1,2},{2,1},{3,0},{4,7},{5,6},{6,5},{7,4},{8,11},{9,10},{10,... | collective-permute-start | bytes 884744 | tf_op jit(solution)/shard_map/ppermute | solution.py:32
  638.1 17.7 %collective-permute-start.3 = (bf16[1,3,3,16384]{3,2,1,0:T(4,128)(2,1)S(1)}, bf16[1,3,3,16384]{3,2,1,0:T(4,128)(2,1)S(1)}, u32[]{:S(2)}, u32[]{:S(2)}) collective-permute-start(bf16[1,3,3,16384]{3,2,1,0:T(4,128)(2,1)S(1)} %bitcast.306), channel_id=1, source_target_pairs={{0,4},{1,5},{2,6},{3,7},{4,0},{5,1},{6,2},{7,3},{8,12},{9,13},{10,... | collective-permute-start | bytes 884744 | tf_op jit(solution)/shard_map/ppermute | solution.py:32
  638.7 35.4 %collective-permute-start.4 = (bf16[1,3,3,16384]{3,2,1,0:T(4,128)(2,1)S(1)}, bf16[1,3,3,16384]{3,2,1,0:T(4,128)(2,1)S(1)}, u32[]{:S(2)}, u32[]{:S(2)}) collective-permute-start(bf16[1,3,3,16384]{3,2,1,0:T(4,128)(2,1)S(1)} %bitcast.305), channel_id=1, source_target_pairs={{0,5},{1,4},{2,7},{3,6},{4,1},{5,0},{6,3},{7,2},{8,13},{9,12},{10,... | collective-permute-start | bytes 884744 | tf_op jit(solution)/shard_map/ppermute | solution.py:32
  641.0 33.3 %collective-permute-start.5 = (bf16[1,3,3,16384]{3,2,1,0:T(4,128)(2,1)S(1)}, bf16[1,3,3,16384]{3,2,1,0:T(4,128)(2,1)S(1)}, u32[]{:S(2)}, u32[]{:S(2)}) collective-permute-start(bf16[1,3,3,16384]{3,2,1,0:T(4,128)(2,1)S(1)} %bitcast.309), channel_id=1, source_target_pairs={{0,6},{1,7},{2,4},{3,5},{4,2},{5,3},{6,0},{7,1},{8,14},{9,15},{10,... | collective-permute-start | bytes 884744 | tf_op jit(solution)/shard_map/ppermute | solution.py:32
  648.3 26.2 %collective-permute-start.6 = (bf16[1,3,3,16384]{3,2,1,0:T(4,128)(2,1)S(1)}, bf16[1,3,3,16384]{3,2,1,0:T(4,128)(2,1)S(1)}, u32[]{:S(2)}, u32[]{:S(2)}) collective-permute-start(bf16[1,3,3,16384]{3,2,1,0:T(4,128)(2,1)S(1)} %bitcast.308), channel_id=1, source_target_pairs={{0,7},{1,6},{2,5},{3,4},{4,3},{5,2},{6,1},{7,0},{8,15},{9,14},{10,... | collective-permute-start | bytes 884744 | tf_op jit(solution)/shard_map/ppermute | solution.py:32
  681.6 5.6 copy-start.41
  715.2 104.4 %reduce-scatter.29.cloned.1.call-start = ((), (), s32[]{:S(2)}) async-start(), calls=%async_computation.22 | async-start | bytes 5308416
  729.9 146.9 %reduce-scatter.21.cloned.1.call-start = ((), (), s32[]{:S(2)}) async-start(), calls=%async_computation.18 | async-start | bytes 5308416 | tf_op jit(solution)/shard_map/reduce_scatter | solution.py:322
  739.7 186.8 %reduce-scatter.27.cloned.1.call-start = ((), (), s32[]{:S(2)}) async-start(), calls=%async_computation.21 | async-start | bytes 245760
  741.5 186.6 %reduce-scatter.25.cloned.1.call-start = ((), (), s32[]{:S(2)}) async-start(), calls=%async_computation.20 | async-start | bytes 737280
  764.4 57.5 %copy-start.23 = (f32[9]{0:T(128)S(1)}, f32[9]{0:T(128)}, u32[]{:S(2)}) copy-start(f32[9]{0:T(128)} %param.33) | copy-start | bytes 112
  764.5 180.5 %reduce-scatter.19.cloned.1.call-start = ((), (), s32[]{:S(2)}) async-start(), calls=%async_computation.17 | async-start | bytes 737280 | tf_op jit(solution)/shard_map/reduce_scatter | solution.py:333
  821.8 146.1 %reduce-scatter.23.cloned.1.call-start = ((), (), s32[]{:S(2)}) async-start(), calls=%async_computation.19 | async-start | bytes 737280 | tf_op jit(solution)/shard_map/reduce_scatter | solution.py:336
  876.9 6.4 copy-start.36
  876.9 6.4 copy-start.37
  876.9 46.8 %copy-start.2 = (f32[512,768]{1,0:T(8,128)S(1)}, f32[512,768]{1,0:T(8,128)}, u32[]{:S(2)}) copy-start(f32[512,768]{1,0:T(8,128)} %copy-done.1) | copy-start | bytes 4718596
  (34 other events, 85.2 us)
Sparse Core Ops, SparseCore 0:
  27.0 35.0 all-gather.4
  64.5 23.9 all-gather.6
  90.4 47.8 all-gather.8
  140.0 55.4 all-gather.10
  355.6 37.7 reduce-scatter.16
  715.3 46.9 reduce-scatter.14
  765.8 53.7 reduce-scatter.28
  823.0 53.7 reduce-scatter.20
  879.7 19.5 reduce-scatter.26
  901.5 20.6 reduce-scatter.24
  924.4 20.5 reduce-scatter.18
  947.1 20.6 reduce-scatter.22
